TPU v7x, 32 devices: a whole 2x2x4 slice. The times are simulated.
32 devices in a mesh: region: 2 (over y), mod: 4 (over z), obs: 4 (over x, core).
Axes of the slice: x: 2, y: 2, z: 4, core: 2. Of those that a mesh axis runs over, the one named last changes fastest.
Arguments:
- model_days: float32 [16384, 128], P(('region', 'mod')), parts along dimension 0, may hold values from -48 to 48
- obs_days: float32 [16384, 128], P(('region', 'obs', 'mod')), parts along dimension 0, may hold values from -48 to 48
Outputs:
- mapped: float32 [16384, 128], P(('region', 'mod', 'obs')), parts along dimension 0
- row_potential: float32 [16384], P(('region', 'mod')), parts along dimension 0
- col_potential: float32 [16384], P(('region', 'obs')), parts along dimension 0
There are 2 independent parts, one for each index of `region`. A program takes and returns all parts, laid end to end along the dimension named above; each array names one. Nothing has to cross between parts.
All inputs are finite; a program needn't handle non-finite values.
Results may differ from a plain program's by a relative error of at most 0.0003.
Values sent between devices are 32-bit elements; how exact they have to be, the bound alone decides.
No kernel may reach another device: no remote copies, remote signals or barrier semaphores. Data moves between devices by JAX's collectives and lax.ppermute only.
A program may use at most 64 MiB of HBM per device.

v0:
```python
import math
import jax
import jax.numpy as jnp
from jax import lax
from jax.sharding import PartitionSpec as P

ITERS = 2
entropy_scale = 0.02


def pair_cost(block_rows, block_square, columns):
    column_square = jnp.sum(columns * columns, axis=1)
    cross = lax.dot_general(
        block_rows,
        columns,
        (((1,), (1,)), ((), ())),
        precision=lax.Precision.HIGHEST,
        preferred_element_type=jnp.float32,
    )
    return (block_square[:, None] + column_square[None, :] - 2.0 * cross) / block_rows.shape[1]


def across_obs(peaks, totals):
    highest = lax.pmax(peaks, "obs")
    summed = lax.psum(totals * jnp.exp(peaks - highest), "obs")
    return highest + jnp.log(summed)


def across_mod(peaks, totals):
    highest = lax.pmax(peaks, "mod")
    summed = lax.psum(totals * jnp.exp(peaks - highest), "mod")
    return highest + jnp.log(summed)


def on_device(model_days, obs_days):
    row_square = jnp.sum(model_days * model_days, axis=1)
    row_count = model_days.shape[0]
    col_count = obs_days.shape[0] * lax.axis_size("mod")
    log_obs = math.log(col_count * lax.axis_size("obs"))
    log_model = math.log(row_count * lax.axis_size("mod"))
    gathered = lax.all_gather(obs_days, "mod", axis=0, tiled=True)
    cost_tile = pair_cost(model_days, row_square, gathered)

    def row_stats(col_potential):
        scores = (col_potential[None, :] - cost_tile) / entropy_scale
        peaks = jnp.max(scores, axis=1)
        return (peaks, jnp.sum(jnp.exp(scores - peaks[:, None]), axis=1))

    col_potential = jnp.zeros((col_count,), jnp.float32)
    for iteration in range(ITERS):
        peaks, totals = row_stats(col_potential)
        row_potential = -entropy_scale * (across_obs(peaks, totals) - log_obs)
        col_scores = (row_potential[:, None] - cost_tile) / entropy_scale
        col_peaks = jnp.max(col_scores, axis=0)
        peaks = col_peaks
        totals = jnp.sum(jnp.exp(col_scores - col_peaks[None, :]), axis=0)
        col_potential = -entropy_scale * (across_mod(peaks, totals) - log_model)
    peaks, totals = row_stats(col_potential)
    final_lse = across_obs(peaks, totals)
    row_potential = -entropy_scale * (final_lse - log_obs)
    weights = jnp.exp((col_potential[None, :] - cost_tile) / entropy_scale - final_lse[:, None])
    partial_map = jnp.dot(
        weights, gathered, precision=lax.Precision.HIGHEST, preferred_element_type=jnp.float32
    )
    summed_map = lax.psum(partial_map, "obs")
    share = row_count // lax.axis_size("obs")
    mapped = lax.dynamic_slice_in_dim(summed_map, lax.axis_index("obs") * share, share, 0)
    return (mapped, row_potential, col_potential)


def solution(mesh):
    in_specs = (P(("region", "mod"), None), P(("region", "obs", "mod"), None))
    out_specs = (P(("region", "mod", "obs"), None), P(("region", "mod")), P(("region", "obs")))
    return jax.shard_map(
        on_device, mesh=mesh, in_specs=in_specs, out_specs=out_specs, check_vma=False
    )
```

profile of v0, /device:TPU:0, one launch (start us, length us, event | category | flops | bytes accessed | tf_op | source)
XLA Modules:
  0.0 285.6 jit_solution(2504910936190339218)
XLA Ops:
  7.2 0.0 all-gather.2.cloned.1.call-start
  7.2 0.7 all-gather.2.cloned.1.call-update
  7.9 0.0 all-reduce.2.cloned.1.call-start
  7.9 1.6 multiply_reduce_fusion.1
  9.5 30.8 %all-gather.2.cloned.1.call-done = f32[2048,128]{1,0:T(8,128)} async-done(((f32[512,128]{1,0:T(8,128)}), f32[2048,128]{1,0:T(8,128)}) %all-gather.2.cloned.1.call-update) | async-done | bytes 1048592 | tf_op jit(solution)/shard_map/all_gather | solution.py:41
  40.3 1.6 multiply_reduce_fusion
  41.9 20.6 %fusion.3 = (f32[2048]{0:T(1024)S(1)}, f32[2048,2048]{0,1:T(8,128)}) fusion(f32[2048,128]{1,0:T(8,128)} %param.2, f32[2048,128]{1,0:T(8,128)} %all-gather.2.cloned.1.call-done, f32[2048]{0:T(1024)S(1)} %multiply_reduce_fusion, f32[2048]{0:T(1024)S(1)} %multiply_reduce_fusion.1), kind=kOutput, calls=%fused_computation.14 | convolution fusion | flops 6471809024 | bytes 18898944 | tf_op jit(solution)/shard_map/dot_general | solution.py:13
  62.5 6.2 %pmax.35 = f32[2048]{0:T(1024)S(1)} all-reduce(f32[2048]{0:T(1024)S(1)} %get-tuple-element.5), channel_id=1, replica_groups=mesh['region'=2,'mod'=4,'obs'=4] {'obs'}, use_global_device_ids=true, to_apply=%region_3.0 | all-reduce | flops 2048 | bytes 16384 | tf_op jit(solution)/shard_map/pmax | solution.py:24
  68.6 9.1 %exponential_reduce_fusion.4 = f32[2048]{0:T(1024)S(1)} fusion(f32[2048,2048]{0,1:T(8,128)} %get-tuple-element.6, f32[2048]{0:T(1024)S(1)} %get-tuple-element.5), kind=kLoop, calls=%fused_computation.11 | loop fusion | flops 16775168 | bytes 16793600 | tf_op jit(solution)/shard_map/reduce_sum | solution.py:47
  77.7 6.4 %psum.42 = f32[2048]{0:T(1024)S(1)} all-reduce(f32[2048]{0:T(1024)S(1)} %exponential_multiply_fusion.4), channel_id=1, replica_groups=mesh['region'=2,'mod'=4,'obs'=4] {'obs'}, use_global_device_ids=true, to_apply=%region_5.0 | all-reduce | flops 2048 | bytes 16384 | tf_op jit(solution)/shard_map/psum | solution.py:25
  84.2 7.5 %fusion.4 = f32[2048]{0:T(1024)S(1)} fusion(f32[2048,2048]{0,1:T(8,128)} %get-tuple-element.6, f32[2048]{0:T(1024)S(1)} %add_multiply_fusion.4), kind=kLoop, calls=%fused_computation.15 | loop fusion | flops 12580864 | bytes 16793600 | tf_op jit(solution)/shard_map/reduce_max | solution.py:54
  91.7 8.0 %exponential_reduce_fusion.3 = f32[2048]{0:T(1024)S(1)} fusion(f32[2048,2048]{0,1:T(8,128)} %get-tuple-element.6, f32[2048]{0:T(1024)S(1)} %fusion.4, f32[2048]{0:T(1024)S(1)} %add_multiply_fusion.4), kind=kLoop, calls=%fused_computation.9 | loop fusion | flops 16775168 | bytes 16801792 | tf_op jit(solution)/shard_map/reduce_sum | solution.py:56
  99.7 11.0 %pmax.36 = f32[2048]{0:T(1024)S(1)} all-reduce(f32[2048]{0:T(1024)S(1)} %fusion.4), channel_id=1, replica_groups=mesh['region'=2,'mod'=4,'obs'=4] {'mod'}, use_global_device_ids=true, to_apply=%region_7.0 | all-reduce | flops 2048 | bytes 16384 | tf_op jit(solution)/shard_map/pmax | solution.py:30
  110.7 8.5 %psum.43 = f32[2048]{0:T(1024)S(1)} all-reduce(f32[2048]{0:T(1024)S(1)} %exponential_multiply_fusion.3), channel_id=1, replica_groups=mesh['region'=2,'mod'=4,'obs'=4] {'mod'}, use_global_device_ids=true, to_apply=%region_9.0 | all-reduce | flops 2048 | bytes 16384 | tf_op jit(solution)/shard_map/psum | solution.py:31
  119.2 7.5 %fusion.5 = f32[2048]{0:T(1024)S(1)} fusion(f32[2048,2048]{0,1:T(8,128)} %get-tuple-element.6, f32[2048]{0:T(1024)S(1)} %add_multiply_fusion.3), kind=kLoop, calls=%fused_computation.16 | loop fusion | flops 12580864 | bytes 16793600 | tf_op jit(solution)/shard_map/reduce_max | solution.py:46
  126.7 8.0 %exponential_reduce_fusion.2 = f32[2048]{0:T(1024)S(1)} fusion(f32[2048,2048]{0,1:T(8,128)} %get-tuple-element.6, f32[2048]{0:T(1024)S(1)} %fusion.5, f32[2048]{0:T(1024)S(1)} %add_multiply_fusion.3), kind=kLoop, calls=%fused_computation.7 | loop fusion | flops 16775168 | bytes 16801792 | tf_op jit(solution)/shard_map/reduce_sum | solution.py:47
  134.7 5.8 %pmax.37 = f32[2048]{0:T(1024)S(1)} all-reduce(f32[2048]{0:T(1024)S(1)} %fusion.5), channel_id=1, replica_groups=mesh['region'=2,'mod'=4,'obs'=4] {'obs'}, use_global_device_ids=true, to_apply=%region_11.0 | all-reduce | flops 2048 | bytes 16384 | tf_op jit(solution)/shard_map/pmax | solution.py:24
  140.5 6.3 %psum.44 = f32[2048]{0:T(1024)S(1)} all-reduce(f32[2048]{0:T(1024)S(1)} %exponential_multiply_fusion.2), channel_id=1, replica_groups=mesh['region'=2,'mod'=4,'obs'=4] {'obs'}, use_global_device_ids=true, to_apply=%region_13.0 | all-reduce | flops 2048 | bytes 16384 | tf_op jit(solution)/shard_map/psum | solution.py:25
  146.8 7.5 %fusion.6 = f32[2048]{0:T(1024)S(1)} fusion(f32[2048,2048]{0,1:T(8,128)} %get-tuple-element.6, f32[2048]{0:T(1024)S(1)} %add_multiply_fusion.2), kind=kLoop, calls=%fused_computation.17 | loop fusion | flops 12580864 | bytes 16793600 | tf_op jit(solution)/shard_map/reduce_max | solution.py:54
  154.4 8.0 %exponential_reduce_fusion.1 = f32[2048]{0:T(1024)S(1)} fusion(f32[2048,2048]{0,1:T(8,128)} %get-tuple-element.6, f32[2048]{0:T(1024)S(1)} %fusion.6, f32[2048]{0:T(1024)S(1)} %add_multiply_fusion.2), kind=kLoop, calls=%fused_computation.5 | loop fusion | flops 16775168 | bytes 16801792 | tf_op jit(solution)/shard_map/reduce_sum | solution.py:56
  162.3 10.2 %pmax.38 = f32[2048]{0:T(1024)S(1)} all-reduce(f32[2048]{0:T(1024)S(1)} %fusion.6), channel_id=1, replica_groups=mesh['region'=2,'mod'=4,'obs'=4] {'mod'}, use_global_device_ids=true, to_apply=%region_15.0 | all-reduce | flops 2048 | bytes 16384 | tf_op jit(solution)/shard_map/pmax | solution.py:30
  172.6 9.0 %psum.45 = f32[2048]{0:T(1024)S(1)} all-reduce(f32[2048]{0:T(1024)S(1)} %exponential_multiply_fusion.1), channel_id=1, replica_groups=mesh['region'=2,'mod'=4,'obs'=4] {'mod'}, use_global_device_ids=true, to_apply=%region_17.0 | all-reduce | flops 2048 | bytes 16384 | tf_op jit(solution)/shard_map/psum | solution.py:31
  181.7 0.0 copy-start.1
  181.7 0.0 copy-start
  181.7 7.6 %fusion.7 = f32[2048]{0:T(1024)S(1)} fusion(f32[2048,2048]{0,1:T(8,128)} %get-tuple-element.6, f32[2048]{0:T(1024)S(1)} %add_multiply_fusion.1), kind=kLoop, calls=%fused_computation.18 | loop fusion | flops 12580864 | bytes 16793600 | tf_op jit(solution)/shard_map/reduce_max | solution.py:46
  189.2 8.0 %exponential_reduce_fusion = f32[2048]{0:T(1024)S(1)} fusion(f32[2048,2048]{0,1:T(8,128)} %get-tuple-element.6, f32[2048]{0:T(1024)S(1)} %fusion.7, f32[2048]{0:T(1024)S(1)} %add_multiply_fusion.1), kind=kLoop, calls=%fused_computation.3 | loop fusion | flops 16775168 | bytes 16801792 | tf_op jit(solution)/shard_map/reduce_sum | solution.py:47
  197.2 5.8 %pmax.39 = f32[2048]{0:T(1024)S(1)} all-reduce(f32[2048]{0:T(1024)S(1)} %fusion.7), channel_id=1, replica_groups=mesh['region'=2,'mod'=4,'obs'=4] {'obs'}, use_global_device_ids=true, to_apply=%region_19.0 | all-reduce | flops 2048 | bytes 16384 | tf_op jit(solution)/shard_map/pmax | solution.py:24
  203.0 6.9 %psum.46 = f32[2048]{0:T(1024)S(1)} all-reduce(f32[2048]{0:T(1024)S(1)} %exponential_multiply_fusion), channel_id=1, replica_groups=mesh['region'=2,'mod'=4,'obs'=4] {'obs'}, use_global_device_ids=true, to_apply=%region_21.0 | all-reduce | flops 2048 | bytes 16384 | tf_op jit(solution)/shard_map/psum | solution.py:25
  209.9 0.6 add_multiply_fusion
  210.5 0.0 copy-done.1
  210.5 0.0 copy-done
  210.5 31.6 %fusion = f32[2048,128]{1,0:T(8,128)} fusion(f32[2048,128]{1,0:T(8,128)S(1)} %copy-done, f32[2048,2048]{0,1:T(8,128)} %get-tuple-element.6, f32[2048]{0:T(1024)S(1)} %get-tuple-element.4, f32[2048]{0:T(1024)S(1)} %add_multiply_fusion.1), kind=kOutput, calls=%fused_computation | convolution fusion | flops 6455033856 | bytes 18890752 | tf_op jit(solution)/shard_map/dot_general | solution.py:62
  242.1 0.0 all-reduce.2.cloned.1.call-update
  242.1 34.9 %all-reduce.2.cloned.1.call-done = f32[2048,128]{1,0:T(8,128)} async-done(((f32[2048,128]{1,0:T(8,128)}), f32[2048,128]{1,0:T(8,128)}) %all-reduce.2.cloned.1.call-update) | async-done | bytes 1048592 | tf_op jit(solution)/shard_map/psum | solution.py:65
  277.0 1.7 constant_dynamic-slice_fusion
  (9 shorter events, 0.1 us)
Async XLA Ops:
  7.2 33.1 %all-gather.2.cloned.1.call-start = ((), (), s32[]{:S(2)}) async-start(), calls=%async_computation | async-start | bytes 1310720 | tf_op jit(solution)/shard_map/all_gather | solution.py:41
  7.9 269.1 %all-reduce.2.cloned.1.call-start = ((), (), s32[]{:S(2)}) async-start(), calls=%async_computation.1 | async-start | bytes 2097152 | tf_op jit(solution)/shard_map/psum | solution.py:65
  181.7 28.9 %copy-start.1 = (f32[2048]{0:T(1024)}, f32[2048]{0:T(1024)S(1)}, u32[]{:S(2)}) copy-start(f32[2048]{0:T(1024)S(1)} %add_multiply_fusion.1) | copy-start | bytes 24580
  181.7 28.8 %copy-start = (f32[2048,128]{1,0:T(8,128)S(1)}, f32[2048,128]{1,0:T(8,128)}, u32[]{:S(2)}) copy-start(f32[2048,128]{1,0:T(8,128)} %all-gather.2.cloned.1.call-done) | copy-start | bytes 3145732
Sparse Core Ops, SparseCore 0:
  9.5 30.6 all-gather.1
  242.2 34.7 all-reduce.1
where the time goes:
time: 286 us
  blocking collectives  76.1 us (27%)
  other arithmetic  74.9 us (26%)
  waiting for transfers between devices  66.4 us (23%)
  matrix products  52.2 us (18%)
  between operations  14.2 us (5%)
    psum x1, waiting for transfers between devices, on_device(): summed_map = lax.psum(partial_map, 'obs')  34.9 us
    dot_general x1, matrix products, on_device(): jnp.dot(weights, gathered, precision=lax.Precision.HIGHEST, preferred_ele...  31.6 us
    all_gather x1, waiting for transfers between devices, on_device(): gathered = lax.all_gather(obs_days, 'mod', axis=0, tiled=True)  30.8 us
    reduce_sum x3, other arithmetic, row_stats(): return (peaks, jnp.sum(jnp.exp(scores - peaks[:, None]), axis=1))  25 us
    pmax x2, blocking collectives, across_mod(): highest = lax.pmax(peaks, 'mod')  21.2 us
    dot_general x1, matrix products, pair_cost(): lax.dot_general(block_rows, columns, (((1,), (1,)), ((), ())), precision=...  20.6 us
    psum x3, blocking collectives, across_obs(): summed = lax.psum(totals * jnp.exp(peaks - highest), 'obs')  19.7 us
    pmax x3, blocking collectives, across_obs(): highest = lax.pmax(peaks, 'obs')  17.7 us
  transfers between devices with their start and end apart: 2, of which 2 were waited for; matrix products, arithmetic and copies ran while one was open for 1% of the time, Pallas kernels for 0%

commit v1 on v0

--- a/solution.py
+++ b/solution.py
@@ -62,7 +62,11 @@
     partial_map = jnp.dot(
         weights, gathered, precision=lax.Precision.HIGHEST, preferred_element_type=jnp.float32
     )
-    summed_map = lax.psum(partial_map, "obs")
+    summed_map = partial_map
+    for hop in (1, 2):
+        summed_map = summed_map + lax.ppermute(
+            summed_map, "obs", [(dev, dev ^ hop) for dev in range(4)]
+        )
     share = row_count // lax.axis_size("obs")
     mapped = lax.dynamic_slice_in_dim(summed_map, lax.axis_index("obs") * share, share, 0)
     return (mapped, row_potential, col_potential)

time: 286 us -> 278 us (0.972)
  waiting for transfers between devices: 66.4 us -> 58.7 us
    psum x1 -> x0, waiting for transfers between devices: 34.9 us -> none  [on_device(): summed_map = lax.psum(partial_map, 'obs')]
    ppermute x0 -> x2, waiting for transfers between devices: none -> 27.2 us  [on_device(): lax.ppermute(summed_map, 'obs', [(dev, dev ^ hop) for dev in range(4)])]
  transfers between devices with their start and end apart: 2 -> 3, of which waited for: 2 -> 3; matrix products, arithmetic and copies ran while one was open for 1% -> 1% of each run, Pallas kernels for 0% -> 0%
where the time goes in v1:
time: 278 us; the launch traced here: 277 us
  blocking collectives  76.1 us (27%)
  other arithmetic  75.7 us (27%)
  waiting for transfers between devices  58.7 us (21%)
  matrix products  51.4 us (18%)
  between operations  14.2 us (5%)
    all_gather x1, waiting for transfers between devices, on_device(): gathered = lax.all_gather(obs_days, 'mod', axis=0, tiled=True)  30.8 us
    dot_general x1, matrix products, on_device(): jnp.dot(weights, gathered, precision=lax.Precision.HIGHEST, preferred_ele...  30.8 us
    ppermute x2, waiting for transfers between devices, on_device(): lax.ppermute(summed_map, 'obs', [(dev, dev ^ hop) for dev in range(4)])  27.2 us
    reduce_sum x3, other arithmetic, row_stats(): return (peaks, jnp.sum(jnp.exp(scores - peaks[:, None]), axis=1))  25 us
    pmax x2, blocking collectives, across_mod(): highest = lax.pmax(peaks, 'mod')  21.2 us
    dot_general x1, matrix products, pair_cost(): lax.dot_general(block_rows, columns, (((1,), (1,)), ((), ())), precision=...  20.6 us
    psum x3, blocking collectives, across_obs(): summed = lax.psum(totals * jnp.exp(peaks - highest), 'obs')  19.7 us
    pmax x3, blocking collectives, across_obs(): highest = lax.pmax(peaks, 'obs')  17.7 us
  transfers between devices with their start and end apart: 3, of which 3 were waited for; matrix products, arithmetic and copies ran while one was open for 1% of the time, Pallas kernels for 0%

profile of v1, /device:TPU:0, one launch (start us, length us, event | category | flops | bytes accessed | tf_op | source)
XLA Modules:
  0.0 277.0 jit_solution(9420427321987654469)
XLA Ops:
  7.2 0.0 all-gather.2.cloned.1.call-start
  7.2 0.7 all-gather.2.cloned.1.call-update
  7.9 1.6 multiply_reduce_fusion.1
  9.5 30.8 %all-gather.2.cloned.1.call-done = f32[2048,128]{1,0:T(8,128)} async-done(((f32[512,128]{1,0:T(8,128)}), f32[2048,128]{1,0:T(8,128)}) %all-gather.2.cloned.1.call-update) | async-done | bytes 1048592 | tf_op jit(solution)/shard_map/all_gather | solution.py:41
  40.3 1.6 multiply_reduce_fusion
  41.9 20.6 %fusion.3 = (f32[2048]{0:T(1024)S(1)}, f32[2048,2048]{0,1:T(8,128)}) fusion(f32[2048,128]{1,0:T(8,128)} %param.2, f32[2048,128]{1,0:T(8,128)} %all-gather.2.cloned.1.call-done, f32[2048]{0:T(1024)S(1)} %multiply_reduce_fusion, f32[2048]{0:T(1024)S(1)} %multiply_reduce_fusion.1), kind=kOutput, calls=%fused_computation.14 | convolution fusion | flops 6471809024 | bytes 18898944 | tf_op jit(solution)/shard_map/dot_general | solution.py:13
  62.5 6.2 %pmax.35 = f32[2048]{0:T(1024)S(1)} all-reduce(f32[2048]{0:T(1024)S(1)} %get-tuple-element.5), channel_id=1, replica_groups=mesh['region'=2,'mod'=4,'obs'=4] {'obs'}, use_global_device_ids=true, to_apply=%region_3.0 | all-reduce | flops 2048 | bytes 16384 | tf_op jit(solution)/shard_map/pmax | solution.py:24
  68.6 9.1 %exponential_reduce_fusion.4 = f32[2048]{0:T(1024)S(1)} fusion(f32[2048,2048]{0,1:T(8,128)} %get-tuple-element.6, f32[2048]{0:T(1024)S(1)} %get-tuple-element.5), kind=kLoop, calls=%fused_computation.11 | loop fusion | flops 16775168 | bytes 16793600 | tf_op jit(solution)/shard_map/reduce_sum | solution.py:47
  77.7 6.4 %psum.35 = f32[2048]{0:T(1024)S(1)} all-reduce(f32[2048]{0:T(1024)S(1)} %exponential_multiply_fusion.4), channel_id=1, replica_groups=mesh['region'=2,'mod'=4,'obs'=4] {'obs'}, use_global_device_ids=true, to_apply=%region_5.0 | all-reduce | flops 2048 | bytes 16384 | tf_op jit(solution)/shard_map/psum | solution.py:25
  84.2 7.5 %fusion.4 = f32[2048]{0:T(1024)S(1)} fusion(f32[2048,2048]{0,1:T(8,128)} %get-tuple-element.6, f32[2048]{0:T(1024)S(1)} %add_multiply_fusion.4), kind=kLoop, calls=%fused_computation.15 | loop fusion | flops 12580864 | bytes 16793600 | tf_op jit(solution)/shard_map/reduce_max | solution.py:54
  91.7 8.0 %exponential_reduce_fusion.3 = f32[2048]{0:T(1024)S(1)} fusion(f32[2048,2048]{0,1:T(8,128)} %get-tuple-element.6, f32[2048]{0:T(1024)S(1)} %fusion.4, f32[2048]{0:T(1024)S(1)} %add_multiply_fusion.4), kind=kLoop, calls=%fused_computation.9 | loop fusion | flops 16775168 | bytes 16801792 | tf_op jit(solution)/shard_map/reduce_sum | solution.py:56
  99.7 11.0 %pmax.36 = f32[2048]{0:T(1024)S(1)} all-reduce(f32[2048]{0:T(1024)S(1)} %fusion.4), channel_id=1, replica_groups=mesh['region'=2,'mod'=4,'obs'=4] {'mod'}, use_global_device_ids=true, to_apply=%region_7.0 | all-reduce | flops 2048 | bytes 16384 | tf_op jit(solution)/shard_map/pmax | solution.py:30
  110.7 8.5 %psum.36 = f32[2048]{0:T(1024)S(1)} all-reduce(f32[2048]{0:T(1024)S(1)} %exponential_multiply_fusion.3), channel_id=1, replica_groups=mesh['region'=2,'mod'=4,'obs'=4] {'mod'}, use_global_device_ids=true, to_apply=%region_9.0 | all-reduce | flops 2048 | bytes 16384 | tf_op jit(solution)/shard_map/psum | solution.py:31
  119.2 7.5 %fusion.5 = f32[2048]{0:T(1024)S(1)} fusion(f32[2048,2048]{0,1:T(8,128)} %get-tuple-element.6, f32[2048]{0:T(1024)S(1)} %add_multiply_fusion.3), kind=kLoop, calls=%fused_computation.16 | loop fusion | flops 12580864 | bytes 16793600 | tf_op jit(solution)/shard_map/reduce_max | solution.py:46
  126.7 8.0 %exponential_reduce_fusion.2 = f32[2048]{0:T(1024)S(1)} fusion(f32[2048,2048]{0,1:T(8,128)} %get-tuple-element.6, f32[2048]{0:T(1024)S(1)} %fusion.5, f32[2048]{0:T(1024)S(1)} %add_multiply_fusion.3), kind=kLoop, calls=%fused_computation.7 | loop fusion | flops 16775168 | bytes 16801792 | tf_op jit(solution)/shard_map/reduce_sum | solution.py:47
  134.7 5.8 %pmax.37 = f32[2048]{0:T(1024)S(1)} all-reduce(f32[2048]{0:T(1024)S(1)} %fusion.5), channel_id=1, replica_groups=mesh['region'=2,'mod'=4,'obs'=4] {'obs'}, use_global_device_ids=true, to_apply=%region_11.0 | all-reduce | flops 2048 | bytes 16384 | tf_op jit(solution)/shard_map/pmax | solution.py:24
  140.5 6.3 %psum.37 = f32[2048]{0:T(1024)S(1)} all-reduce(f32[2048]{0:T(1024)S(1)} %exponential_multiply_fusion.2), channel_id=1, replica_groups=mesh['region'=2,'mod'=4,'obs'=4] {'obs'}, use_global_device_ids=true, to_apply=%region_13.0 | all-reduce | flops 2048 | bytes 16384 | tf_op jit(solution)/shard_map/psum | solution.py:25
  146.8 7.5 %fusion.6 = f32[2048]{0:T(1024)S(1)} fusion(f32[2048,2048]{0,1:T(8,128)} %get-tuple-element.6, f32[2048]{0:T(1024)S(1)} %add_multiply_fusion.2), kind=kLoop, calls=%fused_computation.17 | loop fusion | flops 12580864 | bytes 16793600 | tf_op jit(solution)/shard_map/reduce_max | solution.py:54
  154.4 8.0 %exponential_reduce_fusion.1 = f32[2048]{0:T(1024)S(1)} fusion(f32[2048,2048]{0,1:T(8,128)} %get-tuple-element.6, f32[2048]{0:T(1024)S(1)} %fusion.6, f32[2048]{0:T(1024)S(1)} %add_multiply_fusion.2), kind=kLoop, calls=%fused_computation.5 | loop fusion | flops 16775168 | bytes 16801792 | tf_op jit(solution)/shard_map/reduce_sum | solution.py:56
  162.3 10.2 %pmax.38 = f32[2048]{0:T(1024)S(1)} all-reduce(f32[2048]{0:T(1024)S(1)} %fusion.6), channel_id=1, replica_groups=mesh['region'=2,'mod'=4,'obs'=4] {'mod'}, use_global_device_ids=true, to_apply=%region_15.0 | all-reduce | flops 2048 | bytes 16384 | tf_op jit(solution)/shard_map/pmax | solution.py:30
  172.6 9.0 %psum.38 = f32[2048]{0:T(1024)S(1)} all-reduce(f32[2048]{0:T(1024)S(1)} %exponential_multiply_fusion.1), channel_id=1, replica_groups=mesh['region'=2,'mod'=4,'obs'=4] {'mod'}, use_global_device_ids=true, to_apply=%region_17.0 | all-reduce | flops 2048 | bytes 16384 | tf_op jit(solution)/shard_map/psum | solution.py:31
  181.7 0.0 copy-start.1
  181.7 0.0 copy-start
  181.7 7.6 %fusion.7 = f32[2048]{0:T(1024)S(1)} fusion(f32[2048,2048]{0,1:T(8,128)} %get-tuple-element.6, f32[2048]{0:T(1024)S(1)} %add_multiply_fusion.1), kind=kLoop, calls=%fused_computation.18 | loop fusion | flops 12580864 | bytes 16793600 | tf_op jit(solution)/shard_map/reduce_max | solution.py:46
  189.2 8.0 %exponential_reduce_fusion = f32[2048]{0:T(1024)S(1)} fusion(f32[2048,2048]{0,1:T(8,128)} %get-tuple-element.6, f32[2048]{0:T(1024)S(1)} %fusion.7, f32[2048]{0:T(1024)S(1)} %add_multiply_fusion.1), kind=kLoop, calls=%fused_computation.3 | loop fusion | flops 16775168 | bytes 16801792 | tf_op jit(solution)/shard_map/reduce_sum | solution.py:47
  197.2 5.8 %pmax.39 = f32[2048]{0:T(1024)S(1)} all-reduce(f32[2048]{0:T(1024)S(1)} %fusion.7), channel_id=1, replica_groups=mesh['region'=2,'mod'=4,'obs'=4] {'obs'}, use_global_device_ids=true, to_apply=%region_19.0 | all-reduce | flops 2048 | bytes 16384 | tf_op jit(solution)/shard_map/pmax | solution.py:24
  203.0 6.9 %psum.39 = f32[2048]{0:T(1024)S(1)} all-reduce(f32[2048]{0:T(1024)S(1)} %exponential_multiply_fusion), channel_id=1, replica_groups=mesh['region'=2,'mod'=4,'obs'=4] {'obs'}, use_global_device_ids=true, to_apply=%region_21.0 | all-reduce | flops 2048 | bytes 16384 | tf_op jit(solution)/shard_map/psum | solution.py:25
  209.9 0.6 add_multiply_fusion
  210.5 0.0 copy-done.1
  210.5 0.0 copy-done
  210.5 30.8 %fusion = f32[2048,128]{1,0:T(8,128)S(1)} fusion(f32[2048,128]{1,0:T(8,128)S(1)} %copy-done, f32[2048,2048]{0,1:T(8,128)} %get-tuple-element.6, f32[2048]{0:T(1024)S(1)} %get-tuple-element.4, f32[2048]{0:T(1024)S(1)} %add_multiply_fusion.1), kind=kOutput, calls=%fused_computation | convolution fusion | flops 6455033856 | bytes 18890752 | tf_op jit(solution)/shard_map/dot_general | solution.py:62
  241.3 0.1 collective-permute-start
  241.4 2.6 collective-permute-done
  244.0 0.1 add.60
  244.1 0.7 collective-permute-start.1
  244.9 24.5 %collective-permute-done.1 = f32[2048,128]{1,0:T(8,128)S(1)} collective-permute-done((f32[2048,128]{1,0:T(8,128)S(1)}, f32[2048,128]{1,0:T(8,128)S(1)}, u32[]{:S(2)}, u32[]{:S(2)}) %collective-permute-start.1) | collective-permute-done | bytes 1048608 | tf_op jit(solution)/shard_map/ppermute | solution.py:67
  269.4 0.7 dynamic-slice_add_fusion
  (9 shorter events, 0.1 us)
Async XLA Ops:
  7.2 33.1 %all-gather.2.cloned.1.call-start = ((), (), s32[]{:S(2)}) async-start(), calls=%async_computation | async-start | bytes 1310720 | tf_op jit(solution)/shard_map/all_gather | solution.py:41
  181.7 28.9 %copy-start.1 = (f32[2048]{0:T(1024)}, f32[2048]{0:T(1024)S(1)}, u32[]{:S(2)}) copy-start(f32[2048]{0:T(1024)S(1)} %add_multiply_fusion.1) | copy-start | bytes 24580
  181.7 28.9 %copy-start = (f32[2048,128]{1,0:T(8,128)S(1)}, f32[2048,128]{1,0:T(8,128)}, u32[]{:S(2)}) copy-start(f32[2048,128]{1,0:T(8,128)} %all-gather.2.cloned.1.call-done) | copy-start | bytes 3145732
  241.3 2.7 collective-permute-start
  244.1 25.3 %collective-permute-start.1 = (f32[2048,128]{1,0:T(8,128)S(1)}, f32[2048,128]{1,0:T(8,128)S(1)}, u32[]{:S(2)}, u32[]{:S(2)}) collective-permute-start(f32[2048,128]{1,0:T(8,128)S(1)} %add.60), channel_id=1, source_target_pairs={{0,2},{1,3},{2,0},{3,1},{4,6},{5,7},{6,4},{7,5},{8,10},{9,11},{10,... | collective-permute-start | bytes 3145736 | tf_op jit(solution)/shard_map/ppermute | solution.py:67
Sparse Core Ops, SparseCore 0:
  9.5 30.6 all-gather.1
